TPU v7x, 32 devices: a whole 2x2x4 slice. The times are simulated.
32 devices in a mesh: shard: 4 (over y, x), ctx: 4 (over z), tp: 2 (over core).
Axes of the slice: x: 2, y: 2, z: 4, core: 2. Of those that a mesh axis runs over, the one named last changes fastest.
Arguments:
- tokens: bfloat16 [10240, 768], P(('shard', 'ctx')), may hold values from -6 to 6
- seq_lengths: int32 [4], P('shard'), may hold values from 2240 to 2560
- query_weight: bfloat16 [768, 768], P('shard', 'tp'), may hold values from -0.21875 to 0.21875
- query_bias: bfloat16 [768], P(('shard', 'tp')), may hold values from -0.59765625 to 0.59765625
- key_weight: bfloat16 [768, 768], P('shard', 'tp'), may hold values from -0.21875 to 0.21875
- value_weight: bfloat16 [768, 768], P('shard', 'tp'), may hold values from -0.21875 to 0.21875
- value_bias: bfloat16 [768], P(('shard', 'tp')), may hold values from -0.119628906 to 0.119628906
- output_weight: bfloat16 [768, 768], P('shard', 'tp'), may hold values from -6 to 6
- output_bias: bfloat16 [768], P('shard'), may hold values from -0.59765625 to 0.59765625
- attn_gain: bfloat16 [768], P('shard'), may hold values from 0.5 to 1.5
- attn_shift: bfloat16 [768], P('shard'), may hold values from -0.59765625 to 0.59765625
- inner_weight: bfloat16 [768, 3072], P('shard', 'tp'), may hold values from -0.21875 to 0.21875
- inner_bias: bfloat16 [3072], P(('shard', 'tp')), may hold values from -0.59765625 to 0.59765625
- outer_weight: bfloat16 [768, 3072], P('shard', 'tp'), may hold values from -0.109375 to 0.109375
- outer_bias: bfloat16 [768], P('shard'), may hold values from -0.59765625 to 0.59765625
- final_gain: bfloat16 [768], P('shard'), may hold values from 0.5 to 1.5
- final_shift: bfloat16 [768], P('shard'), may hold values from -0.59765625 to 0.59765625
- upstream: bfloat16 [10240, 768], P(('shard', 'ctx')), may hold values from -6 to 6
Outputs:
- layer_out: bfloat16 [10240, 768], P(('shard', 'ctx'))
- tokens_gradient: float32 [10240, 768], P(('shard', 'ctx'))
- query_weight_gradient: float32 [768, 768], P('shard', 'tp')
- query_bias_gradient: float32 [768], P(('shard', 'tp'))
- key_weight_gradient: float32 [768, 768], P('shard', 'tp')
- value_weight_gradient: float32 [768, 768], P('shard', 'tp')
- value_bias_gradient: float32 [768], P(('shard', 'tp'))
- output_weight_gradient: float32 [768, 768], P('shard', 'tp')
- output_bias_gradient: float32 [768], P('shard')
- attn_gain_gradient: float32 [768], P('shard')
- attn_shift_gradient: float32 [768], P('shard')
- inner_weight_gradient: float32 [768, 3072], P('shard', 'tp')
- inner_bias_gradient: float32 [3072], P(('shard', 'tp'))
- outer_weight_gradient: float32 [768, 3072], P('shard', 'tp')
- outer_bias_gradient: float32 [768], P('shard')
- final_gain_gradient: float32 [768], P('shard')
- final_shift_gradient: float32 [768], P('shard')
All inputs are finite; a program needn't handle non-finite values.
Results may differ from a plain program's by a relative error of at most 0.014.
Values may be sent and summed in bfloat16 or wider, within the bound.
No kernel may reach another device: no remote copies, remote signals or barrier semaphores. Data moves between devices by JAX's collectives and lax.ppermute only.
A program may use at most 128 MiB of HBM per device.

v0:
```python
import jax
import jax.numpy as jnp
from jax import lax
from jax.sharding import PartitionSpec as P

HEAD_DIM = 64
EPSILON = 1e-12


def norm_parts(hidden):
    center = hidden - jnp.mean(hidden, -1, keepdims=True)
    inverse = lax.rsqrt(jnp.mean(center * center, -1, keepdims=True) + EPSILON)
    return (center * inverse, inverse)


def norm_back(gradient, normal_form, inverse, gain):
    scaled = gradient * gain
    inner = (
        scaled
        - jnp.mean(scaled, -1, keepdims=True)
        - normal_form * jnp.mean(scaled * normal_form, -1, keepdims=True)
    )
    return (inner * inverse, jnp.sum(gradient * normal_form, 0), jnp.sum(gradient, 0))


def exact_gelu(values):
    return jax.nn.gelu(values, approximate=False)


def tp_sum(value):
    if lax.axis_size("tp") == 2:
        return value + lax.ppermute(value, "tp", [(0, 1), (1, 0)])
    return lax.psum(value, "tp")


def tp_gather(value):
    if lax.axis_size("tp") == 2:
        other = lax.ppermute(value, "tp", [(0, 1), (1, 0)])
        first = lax.axis_index("tp") == 0
        return jnp.stack([jnp.where(first, value, other), jnp.where(first, other, value)])
    return lax.all_gather(value, "tp")


def on_device(
    tokens,
    seq_lengths,
    query_weight,
    query_bias,
    key_weight,
    value_weight,
    value_bias,
    output_weight,
    output_bias,
    attn_gain,
    attn_shift,
    inner_weight,
    inner_bias,
    outer_weight,
    outer_bias,
    final_gain,
    final_shift,
    upstream,
):
    row_count, model_width = tokens.shape
    tensor_place = lax.axis_index("tp")
    tensor_count = lax.axis_size("tp")
    head_width = query_weight.shape[1]
    hidden_width = inner_weight.shape[1]
    head_count = head_width // HEAD_DIM
    factor = HEAD_DIM ** (-0.5)
    f32 = jnp.float32
    qb = query_bias.shape[0]
    ib = inner_bias.shape[0]
    piece = output_bias.shape[0]
    tp_blocks = tp_gather(jnp.concatenate([query_bias, value_bias, inner_bias]))
    bias_columns = jnp.concatenate(
        [
            tp_blocks[:, :qb].reshape(piece, 1),
            tp_blocks[:, qb : 2 * qb].reshape(piece, 1),
            tp_blocks[:, 2 * qb :].reshape(piece, -1),
        ],
        axis=1,
    )
    shard_columns = jnp.stack(
        [output_bias, attn_gain, attn_shift, outer_bias, final_gain, final_shift], axis=1
    )
    kv_vec_full = lax.all_gather(
        jnp.concatenate([key_weight, value_weight, shard_columns, bias_columns], axis=1),
        "shard",
        axis=0,
        tiled=True,
    )
    query_full = lax.all_gather(query_weight, "shard", axis=0, tiled=True)
    vector_full = kv_vec_full[:, 2 * head_width :]
    key_full = kv_vec_full[:, :head_width]
    value_full = kv_vec_full[:, head_width : 2 * head_width]
    qkv_full = jnp.concatenate([query_full, kv_vec_full[:, : 2 * head_width]], axis=1)
    rest_full = lax.all_gather(
        jnp.concatenate([output_weight, inner_weight, outer_weight], axis=1),
        "shard",
        axis=0,
        tiled=True,
    )
    output_full = rest_full[:, :head_width]
    inner_full = rest_full[:, head_width : head_width + hidden_width]
    outer_full = rest_full[:, head_width + hidden_width :]
    full_vectors = vector_full[:, :6].T.astype(f32)
    outbias_full, gain_first, shift_first, outerbias_full, gain_second, shift_second = full_vectors
    qbias_all = vector_full[:, 6]
    vbias_all = vector_full[:, 7]
    ibias_all = vector_full[:, 8:].reshape(-1)
    query_shift = lax.dynamic_slice_in_dim(qbias_all, tensor_place * head_width, head_width).astype(
        f32
    )
    value_shift = lax.dynamic_slice_in_dim(vbias_all, tensor_place * head_width, head_width).astype(
        f32
    )
    inner_shift = lax.dynamic_slice_in_dim(
        ibias_all, tensor_place * hidden_width, hidden_width
    ).astype(f32)
    projected = jnp.dot(tokens, kv_vec_full[:, : 2 * head_width], preferred_element_type=f32)
    key_local = projected[:, :head_width].astype(jnp.bfloat16)
    value_local = (projected[:, head_width:] + value_shift).astype(jnp.bfloat16)
    query = (jnp.dot(tokens, query_full, preferred_element_type=f32) + query_shift).astype(
        jnp.bfloat16
    )
    chunk_heads = 2 if head_count % 2 == 0 else 1
    chunk_width = chunk_heads * HEAD_DIM
    kv_chunks = []
    for c in range(head_count // chunk_heads):
        columns = slice(c * chunk_width, (c + 1) * chunk_width)
        outgoing = jnp.concatenate([key_local[:, columns], value_local[:, columns]], axis=1)
        kv_chunks.append(lax.all_gather(outgoing, "ctx", axis=0, tiled=True))
    keys = jnp.concatenate([chunk[:, :chunk_width] for chunk in kv_chunks], axis=1)
    values = jnp.concatenate([chunk[:, chunk_width:] for chunk in kv_chunks], axis=1)
    allowed = jnp.arange(keys.shape[0]) < seq_lengths[0]

    def split_heads_of(matrix, count):
        return matrix.reshape(matrix.shape[0], count, HEAD_DIM).transpose(1, 0, 2)

    def split_heads(matrix):
        return split_heads_of(matrix, head_count)

    def join_heads(stacked):
        return stacked.transpose(1, 0, 2).reshape(stacked.shape[1], head_width)

    def scores_of(query_head, key_head):
        scores = jnp.einsum("qd,kd->qk", query_head, key_head, preferred_element_type=f32) * factor
        return jnp.where(allowed[None, :], scores, -1e30)

    def head_forward(triple):
        query_head, key_head, value_head = triple
        scores = scores_of(query_head, key_head)
        highest = jnp.max(scores, -1, keepdims=True)
        shifted = jnp.exp(scores - highest)
        summed = jnp.sum(shifted, -1, keepdims=True)
        portion = (shifted / summed).astype(jnp.bfloat16)
        mixed = jnp.dot(portion, value_head, preferred_element_type=f32)
        return (mixed.astype(jnp.bfloat16), (highest + jnp.log(summed))[:, 0])

    query_heads = split_heads(query)
    key_heads = split_heads(keys)
    value_heads = split_heads(values)
    chunk_outs = []
    for c, chunk in enumerate(kv_chunks):
        heads = slice(c * chunk_heads, (c + 1) * chunk_heads)
        chunk_outs.append(
            lax.map(
                head_forward,
                (
                    query_heads[heads],
                    split_heads_of(chunk[:, :chunk_width], chunk_heads),
                    split_heads_of(chunk[:, chunk_width:], chunk_heads),
                ),
            )
        )
    context_heads = jnp.concatenate([o[0] for o in chunk_outs])
    log_sums = jnp.concatenate([o[1] for o in chunk_outs])
    context = join_heads(context_heads)
    attn_part = jnp.einsum("th,oh->to", context, output_full, preferred_element_type=f32)
    attended = tp_sum(attn_part) + outbias_full
    normal_first, inverse_first = norm_parts(tokens.astype(f32) + attended)
    normed = normal_first * gain_first + shift_first
    normed_low = normed.astype(jnp.bfloat16)
    hidden = jnp.dot(normed_low, inner_full, preferred_element_type=f32) + inner_shift
    active = exact_gelu(hidden).astype(jnp.bfloat16)
    branch_part = jnp.einsum("tf,of->to", active, outer_full, preferred_element_type=f32)
    branch = tp_sum(branch_part) + outerbias_full
    normal_second, inverse_second = norm_parts(normed + branch)
    layer_out = (normal_second * gain_second + shift_second).astype(jnp.bfloat16)
    dres_second, final_gain_part, final_shift_part = norm_back(
        upstream.astype(f32), normal_second, inverse_second, gain_second
    )
    dbranch = dres_second.astype(jnp.bfloat16)
    outer_bias_part = jnp.sum(dbranch.astype(f32), 0)
    outer_weight_part = jnp.einsum("to,tf->of", dbranch, active, preferred_element_type=f32)
    dactive = jnp.dot(dbranch, outer_full, preferred_element_type=f32)
    unused, gelu_pull = jax.vjp(exact_gelu, hidden)
    dhidden = gelu_pull(dactive)[0].astype(jnp.bfloat16)
    inner_weight_part = jnp.einsum("td,tf->df", normed_low, dhidden, preferred_element_type=f32)
    inner_bias_part = jnp.sum(dhidden.astype(f32), 0)
    dnormed_part = jnp.einsum("tf,df->td", dhidden, inner_full, preferred_element_type=f32)
    dnormed = dres_second + tp_sum(dnormed_part)
    dres_first, attn_gain_part, attn_shift_part = norm_back(
        dnormed, normal_first, inverse_first, gain_first
    )
    dattended = dres_first.astype(jnp.bfloat16)
    output_bias_part = jnp.sum(dattended.astype(f32), 0)
    output_weight_part = jnp.einsum("to,th->oh", dattended, context, preferred_element_type=f32)
    dcontext = jnp.dot(dattended, output_full, preferred_element_type=f32).astype(jnp.bfloat16)
    low = jnp.bfloat16
    rows = model_width
    early = jnp.concatenate(
        [
            output_weight_part,
            inner_weight_part,
            outer_weight_part,
            jnp.stack(
                [
                    output_bias_part,
                    attn_gain_part,
                    attn_shift_part,
                    outer_bias_part,
                    final_gain_part,
                    final_shift_part,
                ],
                axis=1,
            ),
            tp_gather(inner_bias_part).reshape(rows, -1),
        ],
        axis=1,
    ).astype(low)
    early_scattered = lax.psum_scatter(early, "shard", scatter_dimension=0, tiled=True)
    local_rows = piece // tensor_count

    def head_backward(quintet):
        query_head, key_head, value_head, dcontext_head, log_sum = quintet
        portion = jnp.exp(scores_of(query_head, key_head) - log_sum[:, None])
        dportion = jnp.einsum("qd,kd->qk", dcontext_head, value_head, preferred_element_type=f32)
        dvalue_head = jnp.einsum(
            "qk,qd->kd", portion.astype(jnp.bfloat16), dcontext_head, preferred_element_type=f32
        )
        centering = jnp.sum(portion * dportion, -1, keepdims=True)
        dscores = (portion * (dportion - centering)).astype(jnp.bfloat16)
        dquery_head = jnp.dot(dscores, key_head, preferred_element_type=f32) * factor
        dkey_head = (
            jnp.einsum("qk,qd->kd", dscores, query_head, preferred_element_type=f32) * factor
        )
        return (dquery_head.astype(jnp.bfloat16), dkey_head, dvalue_head)

    dquery_heads, dkey_heads, dvalue_heads = lax.map(
        head_backward, (query_heads, key_heads, value_heads, split_heads(dcontext), log_sums)
    )
    dquery = join_heads(dquery_heads)
    dkv_partial = jnp.concatenate(
        [join_heads(dkey_heads), join_heads(dvalue_heads)], axis=1
    ).astype(low)
    dkv_partial, early_scattered = lax.optimization_barrier((dkv_partial, early_scattered))
    dkv = lax.psum_scatter(dkv_partial, "ctx", scatter_dimension=0, tiled=True).astype(jnp.bfloat16)
    early_piece = lax.psum(early_scattered, "ctx").astype(f32)
    output_total = early_piece[:, :head_width]
    inner_total = early_piece[:, head_width : head_width + hidden_width]
    outer_total = early_piece[:, head_width + hidden_width : head_width + 2 * hidden_width]
    early_vectors = early_piece[:, head_width + 2 * hidden_width :]
    (
        outbias_total,
        attn_gain_total,
        attn_shift_total,
        outerbias_total,
        final_gain_total,
        final_shift_total,
    ) = early_vectors[:, :6].T
    ibias_total = lax.dynamic_slice_in_dim(
        early_vectors[:, 6:], tensor_place * local_rows, local_rows, 0
    ).reshape(-1)
    dkeys = dkv[:, :head_width]
    dvalues = dkv[:, head_width:]
    dqkv = jnp.concatenate([dquery, dkeys, dvalues], axis=1)
    qkv_weight_part = jnp.einsum("td,th->dh", tokens, dqkv, preferred_element_type=f32)
    query_bias_part = jnp.sum(dquery.astype(f32), 0)
    value_bias_part = jnp.sum(dvalues.astype(f32), 0)
    dinput_part = jnp.einsum("th,dh->td", dqkv, qkv_full, preferred_element_type=f32)
    tokens_gradient = dres_first + tp_sum(dinput_part)
    late = jnp.concatenate(
        [
            qkv_weight_part,
            tp_gather(query_bias_part).reshape(rows, 1),
            tp_gather(value_bias_part).reshape(rows, 1),
        ],
        axis=1,
    ).astype(low)
    late_piece = lax.psum(
        lax.psum_scatter(late, "shard", scatter_dimension=0, tiled=True), "ctx"
    ).astype(f32)
    query_total = late_piece[:, :head_width]
    key_total = late_piece[:, head_width : 2 * head_width]
    value_total = late_piece[:, 2 * head_width : 3 * head_width]
    qbias_total = lax.dynamic_slice_in_dim(
        late_piece[:, 3 * head_width], tensor_place * local_rows, local_rows
    )
    vbias_total = lax.dynamic_slice_in_dim(
        late_piece[:, 3 * head_width + 1], tensor_place * local_rows, local_rows
    )
    return (
        layer_out,
        tokens_gradient,
        query_total,
        qbias_total,
        key_total,
        value_total,
        vbias_total,
        output_total,
        outbias_total,
        attn_gain_total,
        attn_shift_total,
        inner_total,
        ibias_total,
        outer_total,
        outerbias_total,
        final_gain_total,
        final_shift_total,
    )


def solution(mesh):
    placed = (
        P(("shard", "ctx"), None),
        P("shard"),
        P("shard", "tp"),
        P(("shard", "tp")),
        P("shard", "tp"),
        P("shard", "tp"),
        P(("shard", "tp")),
        P("shard", "tp"),
        P("shard"),
        P("shard"),
        P("shard"),
        P("shard", "tp"),
        P(("shard", "tp")),
        P("shard", "tp"),
        P("shard"),
        P("shard"),
        P("shard"),
        P(("shard", "ctx"), None),
    )
    return jax.shard_map(
        on_device,
        mesh=mesh,
        in_specs=placed,
        out_specs=(
            P(("shard", "ctx"), None),
            P(("shard", "ctx"), None),
            P("shard", "tp"),
            P(("shard", "tp")),
            P("shard", "tp"),
            P("shard", "tp"),
            P(("shard", "tp")),
            P("shard", "tp"),
            P("shard"),
            P("shard"),
            P("shard"),
            P("shard", "tp"),
            P(("shard", "tp")),
            P("shard", "tp"),
            P("shard"),
            P("shard"),
            P("shard"),
        ),
        check_vma=False,
    )
```

profile of v0, /device:TPU:0, one launch (start us, length us, event | category | flops | bytes accessed | tf_op | source)
XLA Modules:
  0.0 627.6 jit_solution(12758260347536476679)
XLA Ops:
  16.6 31.7 %all-gather.6.cloned.1.call-done = bf16[768,780]{1,0:T(8,128)(2,1)} async-done(((bf16[192,780]{1,0:T(8,128)(2,1)}), bf16[768,780]{1,0:T(8,128)(2,1)}) %all-gather.6.cloned.1.call-update) | async-done | bytes 1198096 | tf_op jit(solution)/shard_map/all_gather | solution.py:87
  56.0 10.9 %all_gather.18 = bf16[768,384]{1,0:T(8,128)(2,1)S(1)} all-gather(bf16[192,384]{1,0:T(8,128)(2,1)S(1)} %copy-done.38), channel_id=1, replica_groups=mesh['shard'=4,'ctx'=4,'tp'=2] {'shard'}, dimensions={0}, use_global_device_ids=true | all-gather | bytes 737280 | tf_op jit(solution)/shard_map/all_gather | solution.py:93
  69.2 16.3 %all-gather.8.cloned.1.call-done = bf16[2560,256]{0,1:T(8,128)(2,1)} async-done(((bf16[640,256]{0,1:T(8,128)(2,1)}), bf16[2560,256]{0,1:T(8,128)(2,1)}) %all-gather.8.cloned.1.call-update) | async-done | bytes 1310736 | tf_op jit(solution)/shard_map/all_gather | solution.py:133
  89.2 18.7 %while.54 = (s32[]{:T(128)}, bf16[2,640,64]{1,2,0:T(8,128)(2,1)S(1)}, f32[2,640]{1,0:T(2,128)S(1)}, bf16[2,640,64]{2,1,0:T(8,128)(2,1)S(1)}, bf16[2,2560,64]{2,1...) while((s32[]{:T(128)}, ...), condition=%wide.region_3.4_spmd.clone, body=%wide.region_0.3_spmd.clone.sunk | while | flops 439134080 | bytes 50100380 | solution.py:168
  93.9 4.7 fusion.185
  103.3 4.6 fusion.185
  107.9 10.9 %all-gather.10.cloned.1.call-done = bf16[2560,256]{0,1:T(8,128)(2,1)} async-done(((bf16[640,256]{0,1:T(8,128)(2,1)}), bf16[2560,256]{0,1:T(8,128)(2,1)}) %all-gather.10.cloned.1.call-update) | async-done | bytes 1310736 | tf_op jit(solution)/shard_map/all_gather | solution.py:133
  122.4 30.0 %all-gather.12.cloned.1.call-done = bf16[2560,256]{0,1:T(8,128)(2,1)} async-done(((bf16[640,256]{0,1:T(8,128)(2,1)}), bf16[2560,256]{0,1:T(8,128)(2,1)}) %all-gather.12.cloned.1.call-update) | async-done | bytes 1310736 | tf_op jit(solution)/shard_map/all_gather | solution.py:133
  158.0 20.9 %while.55 = (s32[]{:T(128)}, bf16[2,640,64]{1,2,0:T(8,128)(2,1)S(1)}, f32[2,640]{1,0:T(2,128)S(1)}, bf16[2,640,64]{2,1,0:T(8,128)(2,1)}, bf16[2,2560,64]{2,1,0:T...) while((s32[]{:T(128)}, ...), condition=%wide.region_7.8_spmd.clone, body=%wide.region_4.7_spmd.clone.sunk | while | flops 439134080 | bytes 47478912 | solution.py:168
  164.0 4.7 fusion.189
  174.2 4.7 fusion.189
  179.6 21.3 %while.56 = (s32[]{:T(128)}, bf16[2,640,64]{1,2,0:T(8,128)(2,1)S(1)}, f32[2,640]{1,0:T(2,128)S(1)}, bf16[2,640,64]{2,1,0:T(8,128)(2,1)}, bf16[2,2560,64]{2,1,0:T...) while((s32[]{:T(128)}, ...), condition=%wide.region_11.12_spmd.clone, body=%wide.region_8.11_spmd.clone.sunk | while | flops 439134080 | bytes 50100380 | solution.py:168
  202.8 13.1 %all-gather.14.cloned.1.call-done = bf16[768,3456]{1,0:T(8,128)(2,1)} async-done(((bf16[192,3456]{1,0:T(8,128)(2,1)}), bf16[768,3456]{1,0:T(8,128)(2,1)}) %all-gather.14.cloned.1.call-update) | async-done | bytes 5308432 | tf_op jit(solution)/shard_map/all_gather | solution.py:98
  225.1 12.0 %multiply_convert_fusion.1 = (bf16[640,1536]{1,0:T(8,128)(2,1)S(1)}, f32[640,1536]{1,0:T(8,128)}, f32[640,1536]{1,0:T(8,128)}) fusion(f32[1536]{0:T(1024)S(1)} %dynamic-slice_convert_fusion, bf16[768,3456]{1,0:T(8,128)(2,1)S(1)} %bitcast.230, f32[640,768]{1,0:T(8,128)S(1)} %get-tuple-element.416, f32[768]{0:T(1024)S(1)} %get-tuple-element.333, ...), kind=kOutput, calls=%fused_computation.110 | convolution fusion | flops 1577287680 | bytes 14180352 | tf_op jit(solution)/shard_map/dot_general | solution.py:185
  260.0 4.9 copy.92
  267.4 5.1 copy.94
  273.5 5.4 convolution_convert_fusion.2
  293.3 8.9 %concatenate.60 = bf16[768,3466]{1,0:T(8,128)(2,1)} concatenate(bf16[768,384]{1,0:T(8,128)(2,1)S(1)} %copy.95, bf16[768,1536]{1,0:T(8,128)(2,1)S(1)} %copy-done.27, bf16[768,1536]{1,0:T(8,128)(2,1)} %convolution_convert_fusion.1, bf16[768,1]{1,0:T(8,128)(2,1)S(1)} %stack.117, bf16[768,1]{1,0:T(8,128)(2,1)S(1)} %stack.118, bf16[768,1]{1,0:T(8,128)(2,1)S(1)} %stack.119, ...), dimensions={1} | concatenate | bytes 10647552 | tf_op jit(solution)/shard_map/concatenate | solution.py:213
  307.9 85.2 %while.57 = (s32[]{:T(128)}, bf16[6,640,64]{1,2,0:T(8,128)(2,1)}, bf16[6,2560,64]{1,2,0:T(8,128)(2,1)}, bf16[6,2560,64]{1,2,0:T(8,128)(2,1)}, bf16[6,640,64]{2,1...) while((s32[]{:T(128)}, bf16[6,640,64]{1,2,0:T(8,128)(2,1)}, ...), condition=%wide.region_22.23_spmd.clone, body=%wide.region_20.22_spmd.clone.sunk | while | flops 1063569280 | bytes 53189236 | solution.py:251
  397.4 6.3 copy.105
  406.1 70.1 %reduce-scatter.10.cloned.1.call-done = bf16[640,768]{1,0:T(8,128)(2,1)} async-done(((bf16[2560,768]{1,0:T(8,128)(2,1)}), bf16[640,768]{1,0:T(8,128)(2,1)}) %reduce-scatter.10.cloned.1.call-update) | async-done | bytes 983056
  480.9 7.2 %concatenate.63 = bf16[768,1154]{0,1:T(8,128)(2,1)S(1)} concatenate(bf16[768,1152]{0,1:T(8,128)(2,1)} %fusion.92, bf16[768,1]{0,1:T(2,128)(2,1)S(1)} %bitcast.233, bf16[768,1]{0,1:T(2,128)(2,1)S(1)} %bitcast.234), dimensions={1} | concatenate | bytes 3545088 | tf_op jit(solution)/shard_map/concatenate | solution.py:284
  495.1 30.1 %reduce-scatter.12.cloned.1.call-done = bf16[192,1154]{1,0:T(8,128)(2,1)} async-done(((bf16[768,1154]{1,0:T(8,128)(2,1)}), bf16[192,1154]{1,0:T(8,128)(2,1)}) %reduce-scatter.12.cloned.1.call-update) | async-done | bytes 443152
  531.1 79.8 %all-reduce.3.cloned.1.call-done = (bf16[192,1154]{0,1:T(8,128)(2,1)}, bf16[192,3466]{1,0:T(8,128)(2,1)}) async-done(((bf16[192,1154]{0,1:T(8,128)(2,1)}, bf16[192,3466]{1,0:T(8,128)(2,1)}), (bf16[192,1154]{0,1:T(8,128)(2,1)}, bf16[192,3466]{1,0:T(8,128)(2,1)})) %all-reduce.3.cloned.1.call-update) | async-done | bytes 1774096 | tf_op jit(solution)/shard_map/psum | solution.py:292
  (364 shorter events, 250.4 us)
Async XLA Ops:
  7.2 42.4 %copy-start.24 = (bf16[640,768]{1,0:T(8,128)(2,1)S(1)}, bf16[640,768]{1,0:T(8,128)(2,1)}, u32[]{:S(2)}) copy-start(bf16[640,768]{1,0:T(8,128)(2,1)} %param.26) | copy-start | bytes 2949124
  7.2 41.1 %all-gather.6.cloned.1.call-start = ((), (), s32[]{:S(2)}) async-start(), calls=%async_computation.3 | async-start | bytes 1720320 | tf_op jit(solution)/shard_map/all_gather | solution.py:87
  8.1 5.0 collective-permute-start
  16.5 69.0 %all-gather.8.cloned.1.call-start = ((), (), s32[]{:S(2)}) async-start(), calls=%async_computation.4 | async-start | bytes 1638400 | tf_op jit(solution)/shard_map/all_gather | solution.py:133
  53.0 65.7 %all-gather.10.cloned.1.call-start = ((), (), s32[]{:S(2)}) async-start(), calls=%async_computation.5 | async-start | bytes 1638400 | tf_op jit(solution)/shard_map/all_gather | solution.py:133
  53.9 98.6 %all-gather.12.cloned.1.call-start = ((), (), s32[]{:S(2)}) async-start(), calls=%async_computation.6 | async-start | bytes 1638400 | tf_op jit(solution)/shard_map/all_gather | solution.py:133
  54.7 161.2 %all-gather.14.cloned.1.call-start = ((), (), s32[]{:S(2)}) async-start(), calls=%async_computation.7 | async-start | bytes 6635520 | tf_op jit(solution)/shard_map/all_gather | solution.py:98
  56.0 341.4 %reduce-scatter.8.cloned.1.call-start = ((), (), s32[]{:S(2)}) async-start(), calls=%async_computation.8 | async-start | bytes 6881280 | tf_op jit(solution)/shard_map/reduce_scatter | solution.py:233
  68.2 18.7 %copy-start.6 = (bf16[640,6,64]{2,0,1:T(8,128)(2,1)}, bf16[640,6,64]{2,0,1:T(8,128)(2,1)S(1)}, u32[]{:S(2)}) copy-start(bf16[640,6,64]{2,0,1:T(8,128)(2,1)S(1)} %copy.85) | copy-start | bytes 1474564
  120.1 34.5 %copy-start.16 = (bf16[2560,128]{0,1:T(8,128)(2,1)}, bf16[2560,128]{0,1:T(8,128)(2,1)S(1)}, u32[]{:S(2)}) copy-start(bf16[2560,128]{0,1:T(8,128)(2,1)S(1)} %get-tuple-element.432) | copy-start | bytes 1966084
  120.2 34.5 %copy-start.18 = (bf16[2560,128]{0,1:T(8,128)(2,1)}, bf16[2560,128]{0,1:T(8,128)(2,1)S(1)}, u32[]{:S(2)}) copy-start(bf16[2560,128]{0,1:T(8,128)(2,1)S(1)} %get-tuple-element.433) | copy-start | bytes 1966084
  200.9 17.0 %copy-start.11 = (bf16[768,780]{1,0:T(8,128)(2,1)S(1)}, bf16[768,780]{1,0:T(8,128)(2,1)}, u32[]{:S(2)}) copy-start(bf16[768,780]{1,0:T(8,128)(2,1)} %all-gather.6.cloned.1.call-done) | copy-start | bytes 3594244
  217.8 4.2 collective-permute-start.1
  240.1 4.3 collective-permute-start.2
  258.5 27.6 %collective-permute-start.3 = (f32[640,768]{1,0:T(8,128)}, f32[640,768]{1,0:T(8,128)}, u32[]{:S(2)}, u32[]{:S(2)}) collective-permute-start(f32[640,768]{1,0:T(8,128)} %fusion.102), channel_id=1, source_target_pairs={{0,1},{1,0},{2,3},{3,2},{4,5},{5,4},{6,7},{7,6},{8,9},{9,8},{10,11... | collective-permute-start | bytes 5898248 | tf_op jit(solution)/shard_map/ppermute | solution.py:32
  273.1 11.8 %collective-permute-start.4 = (bf16[1536]{0:T(1024)(128)(2,1)S(1)}, bf16[1536]{0:T(1024)(128)(2,1)S(1)}, u32[]{:S(2)}, u32[]{:S(2)}) collective-permute-start(bf16[1536]{0:T(1024)(128)(2,1)S(1)} %get-tuple-element.464), channel_id=1, source_target_pairs={{0,1},{1,0},{2,3},{3,2},{4,5},{5,4},{6,7},{7,6},{8,9},{9,8},{10,11... | collective-permute-start | bytes 9224 | tf_op jit(solution)/shard_map/ppermute | solution.py:38
  302.3 173.9 %reduce-scatter.10.cloned.1.call-start = ((), (), s32[]{:S(2)}) async-start(), calls=%async_computation.9 | async-start | bytes 4915200
  403.7 74.4 %copy-start.26 = (bf16[640,768]{1,0:T(8,128)(2,1)S(1)}, bf16[640,768]{1,0:T(8,128)(2,1)}, u32[]{:S(2)}) copy-start(bf16[640,768]{1,0:T(8,128)(2,1)} %param.26) | copy-start | bytes 2949124
  403.7 121.5 %reduce-scatter.12.cloned.1.call-start = ((), (), s32[]{:S(2)}) async-start(), calls=%async_computation.10 | async-start | bytes 2457600
  404.9 1.2 collective-permute-start.6
  477.9 2.9 collective-permute-start.7
  490.4 120.5 %all-reduce.3.cloned.1.call-start = ((), (), s32[]{:S(2)}) async-start(), calls=%async_computation.11 | async-start | bytes 3940352 | tf_op jit(solution)/shard_map/psum | solution.py:292
  494.6 32.8 %copy-start.5 = (f32[640,768]{1,0:T(8,128)S(1)}, f32[640,768]{1,0:T(8,128)}, u32[]{:S(2)}) copy-start(f32[640,768]{1,0:T(8,128)} %copy-done.3) | copy-start | bytes 5898244
  494.6 32.7 %collective-permute-start.5 = (f32[640,768]{1,0:T(8,128)}, f32[640,768]{1,0:T(8,128)}, u32[]{:S(2)}, u32[]{:S(2)}) collective-permute-start(f32[640,768]{1,0:T(8,128)} %fusion.110), channel_id=1, source_target_pairs={{0,1},{1,0},{2,3},{3,2},{4,5},{5,4},{6,7},{7,6},{8,9},{9,8},{10,11... | collective-permute-start | bytes 5898248 | tf_op jit(solution)/shard_map/ppermute | solution.py:32
  (50 other events, 175.0 us)
Sparse Core Ops, SparseCore 0:
  16.6 31.5 all-gather.5
  53.2 32.2 all-gather.7
  87.1 31.6 all-gather.9
  120.8 31.6 all-gather.11
  154.7 61.1 all-gather.13
  302.4 63.4 reduce-scatter.7
  403.8 72.3 reduce-scatter.9
  490.5 34.6 reduce-scatter.11
  528.3 82.5 all-reduce.2
where the time goes:
time: 633 us; the launch traced here: 628 us
  waiting for transfers between devices  288 us (45%)
  matrix products  155 us (24%)
  local copies, waits for them, and re-layouts  98.7 us (16%)
  other arithmetic  56.9 us (9%)
  between operations  15 us (2%)
  blocking collectives  10.9 us (2%)
    unnamed x11, waiting for transfers between devices  100 us
    psum x1, waiting for transfers between devices, on_device(): lax.psum(lax.psum_scatter(late, 'shard', scatter_dimension=0, tiled=True)...  79.8 us
    all_gather x3, waiting for transfers between devices, on_device(): kv_chunks.append(lax.all_gather(outgoing, 'ctx', axis=0, tiled=True))  57.2 us
    all_gather x1, waiting for transfers between devices, on_device(): lax.all_gather(jnp.concatenate([key_weight, value_weight, shard_columns,...  31.7 us
    dot_general x12, matrix products, scores_of(): jnp.einsum('qd,kd->qk', query_head, key_head, preferred_element_type=f32)  30.3 us
    dot_general x6, matrix products, head_forward(): mixed = jnp.dot(portion, value_head, preferred_element_type=f32)  27.8 us
    unnamed x101, local copies, waits for them, and re-layouts  21.3 us
    reshape x10, local copies, waits for them, and re-layouts, split_heads_of(): return matrix.reshape(matrix.shape[0], count, HEAD_DIM).transpose(1, 0, 2)  19.7 us
  transfers between devices with their start and end apart: 17, of which 11 were waited for; matrix products, arithmetic and copies ran while one was open for 34% of the time, Pallas kernels for 0%

commit v1 on v0

--- a/solution.py
+++ b/solution.py
@@ -130,7 +130,32 @@
     for c in range(head_count // chunk_heads):
         columns = slice(c * chunk_width, (c + 1) * chunk_width)
         outgoing = jnp.concatenate([key_local[:, columns], value_local[:, columns]], axis=1)
-        kv_chunks.append(lax.all_gather(outgoing, "ctx", axis=0, tiled=True))
+
+        def create_sector(vec, along_axis):
+            mid_arr = lax.axis_size(along_axis)
+            aux = lax.axis_index(along_axis)
+            moved, before, even = (mid_arr, aux, vec.shape[0])
+            inbox = [k0 * moved if nth == 0 else k0 for nth, k0 in enumerate(vec.shape)]
+            passed = jnp.zeros(inbox, vec.dtype)
+            now = lax.dynamic_update_slice_in_dim(passed, vec, before * even, axis=0)
+            oldest = z_new = vec
+            for idx in range(1, moved // 2 + 1):
+                oldest = lax.ppermute(
+                    oldest, along_axis, perm=[(nth, (nth + 1) % moved) for nth in range(moved)]
+                )
+                now = lax.dynamic_update_slice_in_dim(
+                    now, oldest, (before - idx) % moved * even, axis=0
+                )
+                if 2 * idx < moved:
+                    z_new = lax.ppermute(
+                        z_new, along_axis, [(nth, (nth - 1) % moved) for nth in range(moved)]
+                    )
+                    now = lax.dynamic_update_slice_in_dim(
+                        now, z_new, (before + idx) % moved * even, axis=0
+                    )
+            return now
+
+        kv_chunks.append(create_sector(outgoing, "ctx"))
     keys = jnp.concatenate([chunk[:, :chunk_width] for chunk in kv_chunks], axis=1)
     values = jnp.concatenate([chunk[:, chunk_width:] for chunk in kv_chunks], axis=1)
     allowed = jnp.arange(keys.shape[0]) < seq_lengths[0]

time: 633 us -> 582 us (0.919)
  waiting for transfers between devices: 288 us -> 213 us
  starting transfers between devices: 2.28 us -> 30.4 us
    all_gather x3 -> x0, waiting for transfers between devices: 57.2 us -> none  [on_device(): kv_chunks.append(lax.all_gather(outgoing, 'ctx', axis=0, tiled=True))]
    ppermute x0 -> x9, starting transfers between devices: none -> 28.3 us  [the longest x6 15.2 us: create_sector(): lax.ppermute(oldest, along_axis, perm=[(nth, (nth + 1) % moved) for nth i...]
    reshape x10 -> x2, local copies, waits for them, and re-layouts: 19.7 us -> 3.18 us  [split_heads_of(): return matrix.reshape(matrix.shape[0], count, HEAD_DIM).transpose(1, 0, 2)]
    all_gather x1, waiting for transfers between devices: 31.7 us -> 16.1 us  [on_device(): lax.all_gather(jnp.concatenate([key_weight, value_weight, shard_columns,...]
    ppermute x0 -> x9, waiting for transfers between devices: none -> 13.4 us  [the longest x6 13.4 us: create_sector(): lax.ppermute(oldest, along_axis, perm=[(nth, (nth + 1) % moved) for nth i...]
    all_gather x1, waiting for transfers between devices: 13.1 us -> 0.01 us  [on_device(): lax.all_gather(jnp.concatenate([output_weight, inner_weight, outer_weight...]
    dynamic_update_slice x0 -> x9, local copies, waits for them, and re-layouts: none -> 9.78 us  [the longest x6 6.98 us: create_sector(): lax.dynamic_update_slice_in_dim(now, oldest, (before - idx) % moved * eve...]
    unnamed x11 -> x8, waiting for transfers between devices: 100 us -> 98.2 us
  transfers between devices with their start and end apart: 17 -> 23, of which waited for: 11 -> 10; matrix products, arithmetic and copies ran while one was open for 34% -> 36% of each run, Pallas kernels for 0% -> 0%
where the time goes in v1:
time: 582 us; the launch traced here: 574 us
  waiting for transfers between devices  213 us (37%)
  matrix products  149 us (26%)
  local copies, waits for them, and re-layouts  94.5 us (16%)
  other arithmetic  55.7 us (10%)
  starting transfers between devices  30.4 us (5%)
  between operations  15.3 us (3%)
  blocking collectives  15.2 us (3%)
    unnamed x8, waiting for transfers between devices  98.2 us
    psum x1, waiting for transfers between devices, on_device(): lax.psum(lax.psum_scatter(late, 'shard', scatter_dimension=0, tiled=True)...  79.7 us
    dot_general x6, matrix products, head_forward(): mixed = jnp.dot(portion, value_head, preferred_element_type=f32)  27.4 us
    dot_general x12, matrix products, scores_of(): jnp.einsum('qd,kd->qk', query_head, key_head, preferred_element_type=f32)  27.1 us
    unnamed x85, local copies, waits for them, and re-layouts  22.4 us
    dot_general x6, matrix products, head_backward(): jnp.dot(dscores, key_head, preferred_element_type=f32) * factor  16.4 us
    all_gather x1, waiting for transfers between devices, on_device(): lax.all_gather(jnp.concatenate([key_weight, value_weight, shard_columns,...  16.1 us
    all_gather x1, blocking collectives, on_device(): query_full = lax.all_gather(query_weight, 'shard', axis=0, tiled=True)  15.2 us
  transfers between devices with their start and end apart: 23, of which 10 were waited for; matrix products, arithmetic and copies ran while one was open for 36% of the time, Pallas kernels for 0%

profile of v1, /device:TPU:0, one launch (start us, length us, event | category | flops | bytes accessed | tf_op | source)
XLA Modules:
  0.0 574.1 jit_solution(2555847300912680493)
XLA Ops:
  19.1 15.2 %all_gather.9 = bf16[768,384]{1,0:T(8,128)(2,1)S(1)} all-gather(bf16[192,384]{1,0:T(8,128)(2,1)S(1)} %copy-done.33), channel_id=1, replica_groups=mesh['shard'=4,'ctx'=4,'tp'=2] {'shard'}, dimensions={0}, use_global_device_ids=true | all-gather | bytes 737280 | tf_op jit(solution)/shard_map/all_gather | solution.py:93
  34.4 16.1 %all-gather.3.cloned.1.call-done = bf16[768,780]{1,0:T(8,128)(2,1)} async-done(((bf16[192,780]{1,0:T(8,128)(2,1)}), bf16[768,780]{1,0:T(8,128)(2,1)}) %all-gather.3.cloned.1.call-update) | async-done | bytes 1198096 | tf_op jit(solution)/shard_map/all_gather | solution.py:87
  68.8 7.0 %collective-permute-start.8 = (bf16[640,256]{0,1:T(8,128)(2,1)S(1)}, bf16[640,256]{0,1:T(8,128)(2,1)S(1)}, u32[]{:S(2)}, u32[]{:S(2)}) collective-permute-start(bf16[640,256]{0,1:T(8,128)(2,1)S(1)} %get-tuple-element.517), channel_id=1, source_target_pairs={{0,6},{2,0},{4,2},{6,4},{1,7},{3,1},{5,3},{7,5},{8,14},{10,8},{12,... | collective-permute-start | bytes 983048 | tf_op jit(solution)/shard_map/ppermute | solution.py:150
  76.8 4.6 collective-permute-done.4
  81.3 5.1 collective-permute-start.3
  88.2 7.3 %collective-permute-done.7 = bf16[640,256]{0,1:T(8,128)(2,1)} collective-permute-done((bf16[640,256]{0,1:T(8,128)(2,1)S(1)}, bf16[640,256]{0,1:T(8,128)(2,1)}, u32[]{:S(2)}, u32[]{:S(2)}) %collective-permute-start.7) | collective-permute-done | bytes 327712 | tf_op jit(solution)/shard_map/ppermute | solution.py:143
  95.4 4.9 collective-permute-start.6
  110.1 20.7 %while.54 = (s32[]{:T(128)}, bf16[2,640,64]{1,2,0:T(8,128)(2,1)S(1)}, f32[2,640]{1,0:T(2,128)}, bf16[2,640,64]{2,1,0:T(8,128)(2,1)S(1)}, bf16[2,2560,64]{1,2,0:T...) while((s32[]{:T(128)}, ...), condition=%wide.region_3.4_spmd.clone, body=%wide.region_0.3_spmd.clone.sunk | while | flops 439134080 | bytes 46823552 | solution.py:193
  115.9 4.6 fusion.185
  126.3 4.6 fusion.185
  137.3 20.2 %while.55 = (s32[]{:T(128)}, bf16[2,640,64]{1,2,0:T(8,128)(2,1)S(1)}, f32[2,640]{1,0:T(2,128)S(1)}, bf16[2,640,64]{2,1,0:T(8,128)(2,1)}, bf16[2,2560,64]{1,2,0:T...) while((s32[]{:T(128)}, ...), condition=%wide.region_7.8_spmd.clone, body=%wide.region_4.7_spmd.clone.sunk | while | flops 439134080 | bytes 49445020 | solution.py:193
  142.9 4.6 fusion.189
  152.9 4.6 fusion.189
  158.3 18.4 %while.56 = (s32[]{:T(128)}, bf16[2,640,64]{1,2,0:T(8,128)(2,1)S(1)}, f32[2,640]{1,0:T(2,128)S(1)}, bf16[2,640,64]{2,1,0:T(8,128)(2,1)S(1)}, bf16[2,2560,64]{1,2...) while((s32[]{:T(128)}, ...), condition=%wide.region_11.12_spmd.clone, body=%wide.region_8.11_spmd.clone.sunk | while | flops 439134080 | bytes 46823552 | solution.py:193
  163.0 4.6 fusion.193
  172.1 4.6 fusion.193
  186.7 12.2 %multiply_convert_fusion.1 = (bf16[640,1536]{1,0:T(8,128)(2,1)S(1)}, f32[640,1536]{1,0:T(8,128)}, f32[640,1536]{1,0:T(8,128)}) fusion(f32[1536]{0:T(1024)S(1)} %dynamic-slice_convert_fusion, bf16[768,3456]{1,0:T(8,128)(2,1)S(1)} %bitcast.244, f32[640,768]{1,0:T(8,128)S(1)} %get-tuple-element.478, f32[768]{0:T(1024)S(1)} %get-tuple-element.395, ...), kind=kOutput, calls=%fused_computation.110 | convolution fusion | flops 1577287680 | bytes 14180352 | tf_op jit(solution)/shard_map/dot_general | solution.py:210
  244.6 8.9 %concatenate.60 = bf16[768,3466]{1,0:T(8,128)(2,1)} concatenate(bf16[768,384]{1,0:T(8,128)(2,1)S(1)} %copy.87, bf16[768,1536]{1,0:T(8,128)(2,1)S(1)} %copy-done.26, bf16[768,1536]{1,0:T(8,128)(2,1)} %convolution_convert_fusion.1, bf16[768,1]{1,0:T(8,128)(2,1)S(1)} %stack.117, bf16[768,1]{1,0:T(8,128)(2,1)S(1)} %stack.118, bf16[768,1]{1,0:T(8,128)(2,1)S(1)} %stack.119, ...), dimensions={1} | concatenate | bytes 10647552 | tf_op jit(solution)/shard_map/concatenate | solution.py:238
  259.3 82.3 %while.57 = (s32[]{:T(128)}, bf16[6,640,64]{1,2,0:T(8,128)(2,1)}, bf16[6,2560,64]{1,2,0:T(8,128)(2,1)}, bf16[6,2560,64]{1,2,0:T(8,128)(2,1)}, bf16[6,640,64]{2,1...) while((s32[]{:T(128)}, bf16[6,640,64]{1,2,0:T(8,128)(2,1)}, ...), condition=%wide.region_22.23_spmd.clone, body=%wide.region_20.22_spmd.clone.sunk | while | flops 1063569280 | bytes 52206196 | solution.py:276
  345.8 6.3 %copy.97 = bf16[2560,768]{1,0:T(8,128)(2,1)} copy(bf16[2560,768]{0,1:T(8,128)(2,1)} %pad_maximum_fusion) | data formatting | bytes 7864320
  354.6 68.0 %reduce-scatter.10.cloned.1.call-done = bf16[640,768]{1,0:T(8,128)(2,1)} async-done(((bf16[2560,768]{1,0:T(8,128)(2,1)}), bf16[640,768]{1,0:T(8,128)(2,1)}) %reduce-scatter.10.cloned.1.call-update) | async-done | bytes 983056
  427.2 7.2 %concatenate.63 = bf16[768,1154]{0,1:T(8,128)(2,1)S(1)} concatenate(bf16[768,1152]{0,1:T(8,128)(2,1)} %fusion.92, bf16[768,1]{0,1:T(2,128)(2,1)S(1)} %bitcast.247, bf16[768,1]{0,1:T(2,128)(2,1)S(1)} %bitcast.248), dimensions={1} | concatenate | bytes 3545088 | tf_op jit(solution)/shard_map/concatenate | solution.py:309
  441.4 30.1 %reduce-scatter.12.cloned.1.call-done = bf16[192,1154]{1,0:T(8,128)(2,1)} async-done(((bf16[768,1154]{1,0:T(8,128)(2,1)}), bf16[192,1154]{1,0:T(8,128)(2,1)}) %reduce-scatter.12.cloned.1.call-update) | async-done | bytes 443152
  477.5 79.7 %all-reduce.3.cloned.1.call-done = (bf16[192,1154]{0,1:T(8,128)(2,1)}, bf16[192,3466]{1,0:T(8,128)(2,1)}) async-done(((bf16[192,1154]{0,1:T(8,128)(2,1)}, bf16[192,3466]{1,0:T(8,128)(2,1)}), (bf16[192,1154]{0,1:T(8,128)(2,1)}, bf16[192,3466]{1,0:T(8,128)(2,1)})) %all-reduce.3.cloned.1.call-update) | async-done | bytes 1774096 | tf_op jit(solution)/shard_map/psum | solution.py:317
  (357 shorter events, 258.2 us)
Async XLA Ops:
  7.2 43.3 %all-gather.3.cloned.1.call-start = ((), (), s32[]{:S(2)}) async-start(), calls=%async_computation.3 | async-start | bytes 1720320 | tf_op jit(solution)/shard_map/all_gather | solution.py:87
  8.0 5.0 collective-permute-start
  16.4 161.1 %all-gather.5.cloned.1.call-start = ((), (), s32[]{:S(2)}) async-start(), calls=%async_computation.4 | async-start | bytes 6635520 | tf_op jit(solution)/shard_map/all_gather | solution.py:98
  19.0 326.8 %reduce-scatter.8.cloned.1.call-start = ((), (), s32[]{:S(2)}) async-start(), calls=%async_computation.5 | async-start | bytes 6881280 | tf_op jit(solution)/shard_map/reduce_scatter | solution.py:258
  54.7 14.1 %collective-permute-start.1 = (bf16[640,256]{0,1:T(8,128)(2,1)S(1)}, bf16[640,256]{0,1:T(8,128)(2,1)}, u32[]{:S(2)}, u32[]{:S(2)}) collective-permute-start(bf16[640,256]{0,1:T(8,128)(2,1)S(1)} %get-tuple-element.513), channel_id=1, source_target_pairs={{0,2},{2,4},{4,6},{6,0},{1,3},{3,5},{5,7},{7,1},{8,10},{10,12},{12... | collective-permute-start | bytes 983048 | tf_op jit(solution)/shard_map/ppermute | solution.py:143
  56.2 45.1 %collective-permute-start.2 = (bf16[640,256]{0,1:T(8,128)(2,1)S(1)}, bf16[640,256]{0,1:T(8,128)(2,1)}, u32[]{:S(2)}, u32[]{:S(2)}) collective-permute-start(bf16[640,256]{0,1:T(8,128)(2,1)S(1)} %get-tuple-element.513), channel_id=1, source_target_pairs={{0,6},{2,0},{4,2},{6,4},{1,7},{3,1},{5,3},{7,5},{8,14},{10,8},{12,... | collective-permute-start | bytes 983048 | tf_op jit(solution)/shard_map/ppermute | solution.py:150
  60.7 20.7 %collective-permute-start.4 = (bf16[640,256]{0,1:T(8,128)(2,1)}, bf16[640,256]{0,1:T(8,128)(2,1)}, u32[]{:S(2)}, u32[]{:S(2)}) collective-permute-start(bf16[640,256]{0,1:T(8,128)(2,1)} %get-tuple-element.515), channel_id=1, source_target_pairs={{0,2},{2,4},{4,6},{6,0},{1,3},{3,5},{5,7},{7,1},{8,10},{10,12},{12... | collective-permute-start | bytes 983048 | tf_op jit(solution)/shard_map/ppermute | solution.py:143
  60.7 45.3 %collective-permute-start.5 = (bf16[640,256]{0,1:T(8,128)(2,1)}, bf16[640,256]{0,1:T(8,128)(2,1)}, u32[]{:S(2)}, u32[]{:S(2)}) collective-permute-start(bf16[640,256]{0,1:T(8,128)(2,1)} %get-tuple-element.515), channel_id=1, source_target_pairs={{0,6},{2,0},{4,2},{6,4},{1,7},{3,1},{5,3},{7,5},{8,14},{10,8},{12,... | collective-permute-start | bytes 983048 | tf_op jit(solution)/shard_map/ppermute | solution.py:150
  67.8 27.7 %collective-permute-start.7 = (bf16[640,256]{0,1:T(8,128)(2,1)S(1)}, bf16[640,256]{0,1:T(8,128)(2,1)}, u32[]{:S(2)}, u32[]{:S(2)}) collective-permute-start(bf16[640,256]{0,1:T(8,128)(2,1)S(1)} %get-tuple-element.517), channel_id=1, source_target_pairs={{0,2},{2,4},{4,6},{6,0},{1,3},{3,5},{5,7},{7,1},{8,10},{10,12},{12... | collective-permute-start | bytes 983048 | tf_op jit(solution)/shard_map/ppermute | solution.py:143
  68.8 39.0 %collective-permute-start.8 = (bf16[640,256]{0,1:T(8,128)(2,1)S(1)}, bf16[640,256]{0,1:T(8,128)(2,1)S(1)}, u32[]{:S(2)}, u32[]{:S(2)}) collective-permute-start(bf16[640,256]{0,1:T(8,128)(2,1)S(1)} %get-tuple-element.517), channel_id=1, source_target_pairs={{0,6},{2,0},{4,2},{6,4},{1,7},{3,1},{5,3},{7,5},{8,14},{10,8},{12,... | collective-permute-start | bytes 983048 | tf_op jit(solution)/shard_map/ppermute | solution.py:150
  81.3 28.0 %collective-permute-start.3 = (bf16[640,256]{0,1:T(8,128)(2,1)}, bf16[640,256]{0,1:T(8,128)(2,1)S(1)}, u32[]{:S(2)}, u32[]{:S(2)}) collective-permute-start(bf16[640,256]{0,1:T(8,128)(2,1)} %collective-permute-done.1), channel_id=1, source_target_pairs={{0,2},{2,4},{4,6},{6,0},{1,3},{3,5},{5,7},{7,1},{8,10},{10,12},{12... | collective-permute-start | bytes 983048 | tf_op jit(solution)/shard_map/ppermute | solution.py:143
  95.4 35.5 %collective-permute-start.6 = (bf16[640,256]{0,1:T(8,128)(2,1)}, bf16[640,256]{0,1:T(8,128)(2,1)}, u32[]{:S(2)}, u32[]{:S(2)}) collective-permute-start(bf16[640,256]{0,1:T(8,128)(2,1)} %collective-permute-done.4), channel_id=1, source_target_pairs={{0,2},{2,4},{4,6},{6,0},{1,3},{3,5},{5,7},{7,1},{8,10},{10,12},{12... | collective-permute-start | bytes 983048 | tf_op jit(solution)/shard_map/ppermute | solution.py:143
  101.3 34.0 %collective-permute-start.9 = (bf16[640,256]{0,1:T(8,128)(2,1)}, bf16[640,256]{0,1:T(8,128)(2,1)}, u32[]{:S(2)}, u32[]{:S(2)}) collective-permute-start(bf16[640,256]{0,1:T(8,128)(2,1)} %collective-permute-done.7), channel_id=1, source_target_pairs={{0,2},{2,4},{4,6},{6,0},{1,3},{3,5},{5,7},{7,1},{8,10},{10,12},{12... | collective-permute-start | bytes 983048 | tf_op jit(solution)/shard_map/ppermute | solution.py:143
  179.5 4.2 collective-permute-start.10
  201.9 4.3 collective-permute-start.11
  221.5 15.7 %collective-permute-start.12 = (f32[640,768]{1,0:T(8,128)}, f32[640,768]{1,0:T(8,128)}, u32[]{:S(2)}, u32[]{:S(2)}) collective-permute-start(f32[640,768]{1,0:T(8,128)} %fusion.102), channel_id=1, source_target_pairs={{0,1},{1,0},{2,3},{3,2},{4,5},{5,4},{6,7},{7,6},{8,9},{9,8},{10,11... | collective-permute-start | bytes 5898248 | tf_op jit(solution)/shard_map/ppermute | solution.py:32
  225.7 10.2 %collective-permute-start.13 = (bf16[1536]{0:T(1024)(128)(2,1)S(1)}, bf16[1536]{0:T(1024)(128)(2,1)S(1)}, u32[]{:S(2)}, u32[]{:S(2)}) collective-permute-start(bf16[1536]{0:T(1024)(128)(2,1)S(1)} %get-tuple-element.532), channel_id=1, source_target_pairs={{0,1},{1,0},{2,3},{3,2},{4,5},{5,4},{6,7},{7,6},{8,9},{9,8},{10,11... | collective-permute-start | bytes 9224 | tf_op jit(solution)/shard_map/ppermute | solution.py:38
  253.5 169.0 %reduce-scatter.10.cloned.1.call-start = ((), (), s32[]{:S(2)}) async-start(), calls=%async_computation.6 | async-start | bytes 4915200
  352.1 72.2 %copy-start.19 = (bf16[640,768]{1,0:T(8,128)(2,1)S(1)}, bf16[640,768]{1,0:T(8,128)(2,1)}, u32[]{:S(2)}) copy-start(bf16[640,768]{1,0:T(8,128)(2,1)} %param.26) | copy-start | bytes 2949124
  352.1 119.4 %reduce-scatter.12.cloned.1.call-start = ((), (), s32[]{:S(2)}) async-start(), calls=%async_computation.7 | async-start | bytes 2457600
  353.4 1.2 collective-permute-start.15
  424.3 2.9 collective-permute-start.16
  436.8 120.4 %all-reduce.3.cloned.1.call-start = ((), (), s32[]{:S(2)}) async-start(), calls=%async_computation.8 | async-start | bytes 3940352 | tf_op jit(solution)/shard_map/psum | solution.py:317
  440.9 32.7 %collective-permute-start.14 = (f32[640,768]{1,0:T(8,128)}, f32[640,768]{1,0:T(8,128)}, u32[]{:S(2)}, u32[]{:S(2)}) collective-permute-start(f32[640,768]{1,0:T(8,128)} %fusion.110), channel_id=1, source_target_pairs={{0,1},{1,0},{2,3},{3,2},{4,5},{5,4},{6,7},{7,6},{8,9},{9,8},{10,11... | collective-permute-start | bytes 5898248 | tf_op jit(solution)/shard_map/ppermute | solution.py:32
  (46 other events, 292.1 us)
Sparse Core Ops, SparseCore 0:
  16.6 33.9 all-gather.2
  52.9 61.8 all-gather.4
  253.7 61.5 reduce-scatter.7
  352.3 70.2 reduce-scatter.9
  436.9 34.6 reduce-scatter.11
  474.5 82.6 all-reduce.2
